TPU v7x, 512 devices: a whole 4x8x8 slice. The times are simulated.
512 devices in a mesh: section: 8 (over z), ctx: 8 (over y_hi, x), tp: 8 (over y_lo, core).
Axes of the slice: x: 4, y: 8 (y_hi: 2, y_lo: 4; y = y_hi * 4 + y_lo), z: 8, core: 2. Of those that a mesh axis runs over, the one named last changes fastest.
Arguments:
- block_order: int32 [16], replicated, may hold values from 0 to 15, each once
- plan: int32 [8], replicated, may hold values from 0 to 1
- q_box: bfloat16 [8, 2, 1408, 8192], P('section', None, 'ctx', 'tp'), may hold values from -8 to 8
- k_box: bfloat16 [8, 2, 1408, 1024], P('section', None, ('ctx', 'tp')), may hold values from -8 to 8
- v_box: bfloat16 [8, 2, 1408, 1024], P('section', None, ('ctx', 'tp')), may hold values from -6 to 6
- grad_out: bfloat16 [8, 1408, 8192], P('section', 'ctx', 'tp'), may hold values from -6 to 6
Outputs:
- attn_out: bfloat16 [8, 1408, 8192], P('section', 'ctx', 'tp')
- grad_q: bfloat16 [8, 1408, 8192], P('section', 'ctx', 'tp')
- grad_k: float32 [8, 1408, 1024], P('section', ('ctx', 'tp'))
- grad_v: float32 [8, 1408, 1024], P('section', ('ctx', 'tp'))
Inputs may be any that keep to these rules, and one draw needn't show every extreme that they name: `block_order`: a permutation: every block sits in exactly one storage slot, slot j covering storage rows j * 88 to (j + 1) * 88 - 1.
All inputs are finite; a program needn't handle non-finite values.
Results may differ from a plain program's by a relative error of at most 0.012.
Values may be sent and summed in bfloat16 or wider, within the bound.
No kernel may reach another device: no remote copies, remote signals or barrier semaphores. Data moves between devices by JAX's collectives and lax.ppermute only.
A program may use at most 64 MiB of HBM per device.

v0:
```python
import jax
import jax.numpy as jnp
from jax import lax
from jax.sharding import PartitionSpec as P

HEAD_DIM = 128
NEG = -1e30


def passed_along(block, axis, distance):
    devices = range(lax.axis_size(axis))
    route = [((i - distance) % len(devices), i) for i in devices]
    return lax.ppermute(block, axis, route)


def body(block_order, plan, q_box, k_box, v_box, grad_out):
    tp_count = lax.axis_size("tp")
    ctx_count = lax.axis_size("ctx")
    section_count = lax.axis_size("section")
    tok_rows = q_box.shape[2]
    kv_rows = k_box.shape[2]
    seq_rows = tok_rows * ctx_count
    block_len = seq_rows // block_order.shape[0]
    head_size = HEAD_DIM
    heads_local = q_box.shape[3] // head_size
    kv_local = k_box.shape[3] // head_size // tp_count
    group = heads_local // kv_local
    kv_width = kv_local * head_size
    scale = head_size ** (-0.5)
    section_rank = lax.axis_index("section")
    receiver = (section_rank + 1) % section_count
    wanted = lax.dynamic_index_in_dim(plan, receiver, 0, keepdims=False)
    q_send = lax.dynamic_index_in_dim(q_box[0], wanted, 0, keepdims=False)
    k_send = lax.dynamic_index_in_dim(k_box[0], wanted, 0, keepdims=False)
    v_send = lax.dynamic_index_in_dim(v_box[0], wanted, 0, keepdims=False)
    kv_send = jnp.stack(
        [k_send.reshape(kv_rows, -1, head_size), v_send.reshape(kv_rows, -1, head_size)], axis=2
    ).reshape(kv_rows, -1)
    queries, kv_rows_in = passed_along((q_send, kv_send), "section", 1)
    cotangent = passed_along(grad_out[0], "section", -1)
    kv_tok = lax.all_to_all(kv_rows_in, "tp", split_axis=1, concat_axis=0, tiled=True)
    kv_full = lax.all_gather(kv_tok, "ctx", axis=0, tiled=True)
    kv_full = kv_full.reshape(seq_rows, kv_local, 2, head_size)
    key_heads = kv_full[:, :, 0, :]
    value_heads = kv_full[:, :, 1, :]
    positions = (
        block_order[:, None] * block_len + jnp.arange(block_len, dtype=jnp.int32)[None, :]
    ).reshape(seq_rows)
    query_pos = lax.dynamic_slice_in_dim(positions, lax.axis_index("ctx") * tok_rows, tok_rows)
    visible = (positions[None, :] <= query_pos[:, None])[None, None]
    q4 = queries.reshape(tok_rows, kv_local, group, head_size)
    do4 = cotangent.reshape(tok_rows, kv_local, group, head_size)
    scores = jnp.einsum("qgjd,kgd->gjqk", q4, key_heads, preferred_element_type=jnp.float32) * scale
    scores = jnp.where(visible, scores, NEG)
    top_score = jnp.max(scores, axis=-1, keepdims=True)
    totals = jnp.sum(jnp.where(visible, jnp.exp(scores - top_score), 0.0), axis=-1, keepdims=True)
    log_total = top_score + jnp.log(totals)
    probs = jnp.where(visible, jnp.exp(scores - log_total), 0.0)
    probs_low = probs.astype(jnp.bfloat16)
    attended = jnp.einsum(
        "gjqk,kgd->qgjd", probs_low, value_heads, preferred_element_type=jnp.float32
    )
    delta = jnp.sum(do4.astype(jnp.float32) * attended, axis=-1)
    dprobs = jnp.einsum("qgjd,kgd->gjqk", do4, value_heads, preferred_element_type=jnp.float32)
    dscores = (probs * (dprobs - jnp.transpose(delta, (1, 2, 0))[..., None])).astype(jnp.bfloat16)
    q_grad = (
        jnp.einsum("gjqk,kgd->qgjd", dscores, key_heads, preferred_element_type=jnp.float32) * scale
    ).astype(jnp.bfloat16)
    key_grad = jnp.einsum("gjqk,qgjd->kgd", dscores, q4, preferred_element_type=jnp.float32) * scale
    value_grad = jnp.einsum("gjqk,qgjd->kgd", probs_low, do4, preferred_element_type=jnp.float32)
    attended_flat = attended.astype(jnp.bfloat16).reshape(tok_rows, heads_local * head_size)
    q_grad_flat = q_grad.reshape(tok_rows, heads_local * head_size)
    grad_terms = jnp.stack([key_grad, value_grad], axis=2).reshape(seq_rows, 2 * kv_width)
    own_grads = lax.psum_scatter(grad_terms, "ctx", scatter_dimension=0, tiled=True)
    tok_grads = lax.all_to_all(own_grads, "tp", split_axis=0, concat_axis=1, tiled=True)
    tok_grads = tok_grads.reshape(kv_rows, -1, 2, head_size)
    k_grad_tokens = tok_grads[:, :, 0, :].reshape(kv_rows, -1)
    v_grad_tokens = tok_grads[:, :, 1, :].reshape(kv_rows, -1)
    return (attended_flat[None], q_grad_flat[None], k_grad_tokens[None], v_grad_tokens[None])


def solution(mesh):
    in_specs = (
        P(),
        P(),
        P("section", None, "ctx", "tp"),
        P("section", None, ("ctx", "tp"), None),
        P("section", None, ("ctx", "tp"), None),
        P("section", "ctx", "tp"),
    )
    out_specs = (
        P("section", "ctx", "tp"),
        P("section", "ctx", "tp"),
        P("section", ("ctx", "tp"), None),
        P("section", ("ctx", "tp"), None),
    )
    return jax.shard_map(body, mesh=mesh, in_specs=in_specs, out_specs=out_specs, check_vma=False)
```

profile of v0, /device:TPU:1, one launch (start us, length us, event | category | flops | bytes accessed | tf_op | source)
XLA Modules:
  0.0 212.7 jit_solution(3541561579943129193)
XLA Ops:
  7.2 11.6 %collective-permute-start.2 = (bf16[176,1024]{1,0:T(8,128)(2,1)}, bf16[176,1024]{1,0:T(8,128)(2,1)S(1)}, u32[]{:S(2)}, u32[]{:S(2)}) collective-permute-start(bf16[176,1024]{1,0:T(8,128)(2,1)} %bitcast.163), channel_id=1, source_target_pairs={{64,0},{128,64},{192,128},{256,192},{320,256},{384,320},{448,384},... | collective-permute-start | bytes 1081352 | tf_op jit(solution)/shard_map/ppermute | solution.py:13
  18.8 1.2 dynamic_slice.18
  22.0 1.5 dynamic-slice_reduce_fusion
  23.7 1.9 collective-permute-start
  25.6 0.8 dynamic-slice_bitcast_fusion
  26.4 1.9 collective-permute-start.1
  29.2 1.0 collective-permute-done
  31.0 7.0 %all-to-all-start = ((bf16[22,8,256]{2,0,1:T(8,128)(2,1)}), bf16[22,8,256]{2,0,1:T(8,128)(2,1)S(1)}, u32[]{:S(2)}, u32[]{:S(2)}) async-start(bf16[22,8,256]{2,0,1:T(8,128)(2,1)} %copy.27), calls=%async_computation | async-start | bytes 196608 | tf_op jit(solution)/shard_map/all_to_all | solution.py:41
  38.2 5.1 %all-to-all-done = bf16[22,8,256]{2,0,1:T(8,128)(2,1)S(1)} async-done(((bf16[22,8,256]{2,0,1:T(8,128)(2,1)}), bf16[22,8,256]{2,0,1:T(8,128)(2,1)S(1)}, u32[]{:S(2)}, u32[]{:S(2)}) %all-to-all-start) | async-done | bytes 90144 | tf_op jit(solution)/shard_map/all_to_all | solution.py:41
  43.3 41.5 %all_gather.3 = bf16[1408,256]{1,0:T(8,128)(2,1)S(1)} all-gather(bf16[176,256]{1,0:T(8,128)(2,1)S(1)} %all_to_all.29), channel_id=1, replica_groups=mesh['section'=8,'ctx'=8,'tp'=8] {'ctx'}, dimensions={0}, use_global_device_ids=true | all-gather | bytes 811008 | tf_op jit(solution)/shard_map/all_gather | solution.py:42
  85.4 2.0 fusion.30
  87.4 2.0 select_reduce_fusion
  89.5 1.8 fusion.18
  91.3 2.7 %fusion.6 = bf16[8,176,1408]{2,1,0:T(8,128)(2,1)S(1)} fusion(f32[8,176]{1,0:T(8,128)S(1)} %bitcast.162, f32[1,8,176,1408]{3,2,1,0:T(8,128)S(1)} %get-tuple-element.13, f32[8,176]{1,0:T(8,128)S(1)} %log_add_fusion, pred[176,1408]{1,0:T(8,128)(4,1)S(1)} %broadcast_compare_fusion, bf16[1408,1,2,128]{0,3,2,1:T(8,128)(2,1)S(1)} %bitcast.146, ...), kind=kOutput, calls=%fused_computation.10 | convolution fusion | flops 517423104 | bytes 12879872 | tf_op jit(solution)/shard_map/qgjd,kgd->gjqk/dot_general | solution.py:64
  94.0 0.9 fusion.13
  94.9 1.7 convolution_bitcast_fusion
  96.7 1.5 copy.38
  98.3 0.9 broadcast_in_dim_reshape.7
  99.2 90.8 %reduce-scatter.2.cloned.1.call-done = f32[176,256]{1,0:T(8,128)} async-done(((f32[1408,256]{1,0:T(8,128)}), f32[176,256]{1,0:T(8,128)}) %reduce-scatter.2.cloned.1.call-update) | async-done | bytes 180240 | tf_op jit(solution)/shard_map/reduce_scatter | solution.py:74
  190.0 1.6 all_to_all.30
  191.6 7.0 %all-to-all-start.1 = ((f32[8,22,256]{2,1,0:T(8,128)}), f32[8,22,256]{2,1,0:T(8,128)S(1)}, u32[]{:S(2)}, u32[]{:S(2)}) async-start(f32[8,22,256]{2,1,0:T(8,128)} %all_to_all.30), calls=%async_computation.2 | async-start | bytes 393216 | tf_op jit(solution)/shard_map/all_to_all | solution.py:75
  198.6 3.3 %fusion.17 = bf16[176,1,8,128]{3,0,2,1:T(8,128)(2,1)S(1)} fusion(bf16[8,176,1408]{2,1,0:T(8,128)(2,1)} %copy-done.1, bf16[1408,1,2,128]{0,3,2,1:T(8,128)(2,1)S(1)} %bitcast.147), kind=kOutput, calls=%fused_computation.19 | convolution fusion | flops 507871232 | bytes 4685824 | tf_op jit(solution)/shard_map/gjqk,kgd->qgjd/dot_general | solution.py:67
  202.0 0.9 broadcast_in_dim_reshape.8
  202.9 2.2 %all-to-all-done.1 = f32[8,22,256]{2,1,0:T(8,128)S(1)} async-done(((f32[8,22,256]{2,1,0:T(8,128)}), f32[8,22,256]{2,1,0:T(8,128)S(1)}, u32[]{:S(2)}, u32[]{:S(2)}) %all-to-all-start.1) | async-done | bytes 180256 | tf_op jit(solution)/shard_map/all_to_all | solution.py:75
  (34 shorter events, 3.6 us)
Async XLA Ops:
  7.2 18.5 %copy-start = (bf16[1,2,176,1024]{3,2,1,0:T(8,128)(2,1)S(1)}, bf16[1,2,176,1024]{3,2,1,0:T(8,128)(2,1)}, u32[]{:S(2)}) copy-start(bf16[1,2,176,1024]{3,2,1,0:T(8,128)(2,1)} %param.8) | copy-start | bytes 2162692
  7.2 78.0 %collective-permute-start.2 = (bf16[176,1024]{1,0:T(8,128)(2,1)}, bf16[176,1024]{1,0:T(8,128)(2,1)S(1)}, u32[]{:S(2)}, u32[]{:S(2)}) collective-permute-start(bf16[176,1024]{1,0:T(8,128)(2,1)} %bitcast.163), channel_id=1, source_target_pairs={{64,0},{128,64},{192,128},{256,192},{320,256},{384,320},{448,384},... | collective-permute-start | bytes 1081352 | tf_op jit(solution)/shard_map/ppermute | solution.py:13
  23.7 6.6 %collective-permute-start = (bf16[22,2048]{1,0:T(8,128)(2,1)S(1)}, bf16[22,2048]{1,0:T(8,128)(2,1)S(1)}, u32[]{:S(2)}, u32[]{:S(2)}) collective-permute-start(bf16[22,2048]{1,0:T(8,128)(2,1)S(1)} %reshape.167), channel_id=1, source_target_pairs={{448,0},{0,64},{64,128},{128,192},{192,256},{256,320},{320,384},{3... | collective-permute-start | bytes 270344 | tf_op jit(solution)/shard_map/ppermute | solution.py:13
  26.4 59.0 %collective-permute-start.1 = (bf16[176,1024]{1,0:T(8,128)(2,1)}, bf16[176,1024]{1,0:T(8,128)(2,1)S(1)}, u32[]{:S(2)}, u32[]{:S(2)}) collective-permute-start(bf16[176,1024]{1,0:T(8,128)(2,1)} %dynamic-slice_bitcast_fusion), channel_id=1, source_target_pairs={{448,0},{0,64},{64,128},{128,192},{192,256},{256,320},{320,384},{3... | collective-permute-start | bytes 1081352 | tf_op jit(solution)/shard_map/ppermute | solution.py:13
  31.0 12.3 %all-to-all-start = ((bf16[22,8,256]{2,0,1:T(8,128)(2,1)}), bf16[22,8,256]{2,0,1:T(8,128)(2,1)S(1)}, u32[]{:S(2)}, u32[]{:S(2)}) async-start(bf16[22,8,256]{2,0,1:T(8,128)(2,1)} %copy.27), calls=%async_computation | async-start | bytes 196608 | tf_op jit(solution)/shard_map/all_to_all | solution.py:41
  37.9 152.1 %reduce-scatter.2.cloned.1.call-start = ((), (), s32[]{:S(2)}) async-start(), calls=%async_computation.3 | async-start | bytes 1622016 | tf_op jit(solution)/shard_map/reduce_scatter | solution.py:74
  94.0 2.6 %copy-start.1 = (bf16[8,176,1408]{2,1,0:T(8,128)(2,1)}, bf16[8,176,1408]{2,1,0:T(8,128)(2,1)S(1)}, u32[]{:S(2)}) copy-start(bf16[8,176,1408]{2,1,0:T(8,128)(2,1)S(1)} %fusion.6) | copy-start | bytes 11894788
  191.6 13.5 %all-to-all-start.1 = ((f32[8,22,256]{2,1,0:T(8,128)}), f32[8,22,256]{2,1,0:T(8,128)S(1)}, u32[]{:S(2)}, u32[]{:S(2)}) async-start(f32[8,22,256]{2,1,0:T(8,128)} %all_to_all.30), calls=%async_computation.2 | async-start | bytes 393216 | tf_op jit(solution)/shard_map/all_to_all | solution.py:75
Sparse Core Ops, SparseCore 0:
  98.4 91.6 reduce-scatter.1
where the time goes:
time: 213 us
  waiting for transfers between devices  99.2 us (47%)
  blocking collectives  41.5 us (19%)
  starting transfers between devices  29.4 us (14%)
  between operations  16.2 us (8%)
  matrix products  12.3 us (6%)
  local copies, waits for them, and re-layouts  10.9 us (5%)
  other arithmetic  3.13 us (1%)
    reduce_scatter x1, waiting for transfers between devices, body(): lax.psum_scatter(grad_terms, 'ctx', scatter_dimension=0, tiled=True)  90.8 us
    all_gather x1, blocking collectives, body(): kv_full = lax.all_gather(kv_tok, 'ctx', axis=0, tiled=True)  41.5 us
    ppermute x3, starting transfers between devices, passed_along(): return lax.ppermute(block, axis, route)  15.4 us
    all_to_all x1, starting transfers between devices, body(): lax.all_to_all(kv_rows_in, 'tp', split_axis=1, concat_axis=0, tiled=True)  6.98 us
    all_to_all x1, starting transfers between devices, body(): lax.all_to_all(own_grads, 'tp', split_axis=0, concat_axis=1, tiled=True)  6.96 us
    all_to_all x1, waiting for transfers between devices, body(): lax.all_to_all(kv_rows_in, 'tp', split_axis=1, concat_axis=0, tiled=True)  5.15 us
  transfers between devices with their start and end apart: 6, of which 4 were waited for; matrix products, arithmetic and copies ran while one was open for 5% of the time, Pallas kernels for 0%

commit v1 on v0

--- a/solution.py
+++ b/solution.py
@@ -72,7 +72,10 @@
     q_grad_flat = q_grad.reshape(tok_rows, heads_local * head_size)
     grad_terms = jnp.stack([key_grad, value_grad], axis=2).reshape(seq_rows, 2 * kv_width)
     own_grads = lax.psum_scatter(grad_terms, "ctx", scatter_dimension=0, tiled=True)
-    tok_grads = lax.all_to_all(own_grads, "tp", split_axis=0, concat_axis=1, tiled=True)
+    tok_grads = jnp.concatenate(
+        lax.all_to_all(jnp.stack(jnp.split(own_grads, lax.axis_size("tp"), axis=0)), "tp", 0, 0),
+        axis=1,
+    )
     tok_grads = tok_grads.reshape(kv_rows, -1, 2, head_size)
     k_grad_tokens = tok_grads[:, :, 0, :].reshape(kv_rows, -1)
     v_grad_tokens = tok_grads[:, :, 1, :].reshape(kv_rows, -1)

time: 213 us -> 215 us (level)
    reduce_scatter x1 -> x0, waiting for transfers between devices: 90.8 us -> none  [body(): lax.psum_scatter(grad_terms, 'ctx', scatter_dimension=0, tiled=True)]
    unnamed x1 -> x2, waiting for transfers between devices: 0.02 us -> 90.8 us
    unnamed x9 -> x25, local copies, waits for them, and re-layouts: 0.24 us -> 2.77 us
where the time goes in v1:
time: 215 us; the launch traced here: 214 us
  waiting for transfers between devices  99.2 us (46%)
  blocking collectives  41.5 us (19%)
  starting transfers between devices  29.4 us (14%)
  between operations  16.3 us (8%)
  matrix products  12.3 us (6%)
  local copies, waits for them, and re-layouts  12.2 us (6%)
  other arithmetic  3.13 us (1%)
    unnamed x2, waiting for transfers between devices  90.8 us
    all_gather x1, blocking collectives, body(): kv_full = lax.all_gather(kv_tok, 'ctx', axis=0, tiled=True)  41.5 us
    ppermute x3, starting transfers between devices, passed_along(): return lax.ppermute(block, axis, route)  15.4 us
    all_to_all x1, starting transfers between devices, body(): lax.all_to_all(kv_rows_in, 'tp', split_axis=1, concat_axis=0, tiled=True)  6.98 us
    all_to_all x1, starting transfers between devices, body(): lax.all_to_all(jnp.stack(jnp.split(own_grads, lax.axis_size('tp'), axis=0...  6.96 us
    all_to_all x1, waiting for transfers between devices, body(): lax.all_to_all(kv_rows_in, 'tp', split_axis=1, concat_axis=0, tiled=True)  5.15 us
  transfers between devices with their start and end apart: 6, of which 4 were waited for; matrix products, arithmetic and copies ran while one was open for 5% of the time, Pallas kernels for 0%

profile of v1, /device:TPU:1, one launch (start us, length us, event | category | flops | bytes accessed | tf_op | source)
XLA Modules:
  0.0 214.1 jit_solution(7100270074335350858)
XLA Ops:
  7.2 11.6 %collective-permute-start.2 = (bf16[176,1024]{1,0:T(8,128)(2,1)}, bf16[176,1024]{1,0:T(8,128)(2,1)S(1)}, u32[]{:S(2)}, u32[]{:S(2)}) collective-permute-start(bf16[176,1024]{1,0:T(8,128)(2,1)} %bitcast.180), channel_id=1, source_target_pairs={{64,0},{128,64},{192,128},{256,192},{320,256},{384,320},{448,384},... | collective-permute-start | bytes 1081352 | tf_op jit(solution)/shard_map/ppermute | solution.py:13
  18.8 1.2 dynamic_slice.18
  22.0 1.5 dynamic-slice_reduce_fusion
  23.7 1.9 collective-permute-start
  26.4 1.9 collective-permute-start.1
  29.2 1.0 collective-permute-done
  31.0 7.0 %all-to-all-start = ((bf16[22,8,256]{2,0,1:T(8,128)(2,1)}), bf16[22,8,256]{2,0,1:T(8,128)(2,1)S(1)}, u32[]{:S(2)}, u32[]{:S(2)}) async-start(bf16[22,8,256]{2,0,1:T(8,128)(2,1)} %copy.96), calls=%async_computation | async-start | bytes 196608 | tf_op jit(solution)/shard_map/all_to_all | solution.py:41
  38.2 5.1 %all-to-all-done = bf16[22,8,256]{2,0,1:T(8,128)(2,1)S(1)} async-done(((bf16[22,8,256]{2,0,1:T(8,128)(2,1)}), bf16[22,8,256]{2,0,1:T(8,128)(2,1)S(1)}, u32[]{:S(2)}, u32[]{:S(2)}) %all-to-all-start) | async-done | bytes 90144 | tf_op jit(solution)/shard_map/all_to_all | solution.py:41
  43.3 41.5 %all_gather.3 = bf16[1408,256]{1,0:T(8,128)(2,1)S(1)} all-gather(bf16[176,256]{1,0:T(8,128)(2,1)S(1)} %all_to_all.20), channel_id=1, replica_groups=mesh['section'=8,'ctx'=8,'tp'=8] {'ctx'}, dimensions={0}, use_global_device_ids=true | all-gather | bytes 811008 | tf_op jit(solution)/shard_map/all_gather | solution.py:42
  85.4 2.0 fusion.31
  87.4 2.0 select_reduce_fusion
  89.5 1.8 fusion.18
  91.3 2.7 %fusion.6 = bf16[8,176,1408]{2,1,0:T(8,128)(2,1)S(1)} fusion(f32[8,176]{1,0:T(8,128)S(1)} %bitcast.179, f32[1,8,176,1408]{3,2,1,0:T(8,128)S(1)} %get-tuple-element.21, f32[8,176]{1,0:T(8,128)S(1)} %log_add_fusion, pred[176,1408]{1,0:T(8,128)(4,1)S(1)} %broadcast_compare_fusion, bf16[1408,1,2,128]{0,3,2,1:T(8,128)(2,1)S(1)} %bitcast.164, ...), kind=kOutput, calls=%fused_computation.10 | convolution fusion | flops 517423104 | bytes 12879872 | tf_op jit(solution)/shard_map/qgjd,kgd->gjqk/dot_general | solution.py:64
  94.0 0.9 fusion.13
  94.9 1.7 convolution_bitcast_fusion
  96.7 1.5 copy.109
  98.3 0.9 broadcast_in_dim_reshape.7
  99.2 90.8 %reduce-scatter.4.cloned.1.call-done = f32[176,256]{1,0:T(8,128)} async-done(((f32[1408,256]{1,0:T(8,128)}), f32[176,256]{1,0:T(8,128)}) %reduce-scatter.4.cloned.1.call-update) | async-done | bytes 180240
  190.0 0.9 fusion.30
  192.0 1.0 copy.107
  193.0 7.0 %all-to-all-start.1 = ((f32[8,22,256]{2,1,0:T(8,128)}), f32[8,22,256]{2,1,0:T(8,128)S(1)}, u32[]{:S(2)}, u32[]{:S(2)}) async-start(f32[8,22,256]{2,1,0:T(8,128)} %copy.107), calls=%async_computation.1 | async-start | bytes 393216 | tf_op jit(solution)/shard_map/all_to_all | solution.py:76
  200.0 3.3 %fusion.17 = bf16[176,1,8,128]{3,0,2,1:T(8,128)(2,1)S(1)} fusion(bf16[8,176,1408]{2,1,0:T(8,128)(2,1)} %copy-done.1, bf16[1408,1,2,128]{0,3,2,1:T(8,128)(2,1)S(1)} %bitcast.165), kind=kOutput, calls=%fused_computation.19 | convolution fusion | flops 507871232 | bytes 4685824 | tf_op jit(solution)/shard_map/gjqk,kgd->qgjd/dot_general | solution.py:67
  203.4 0.9 broadcast_in_dim_reshape.8
  204.3 2.2 %all-to-all-done.1 = f32[8,22,256]{2,1,0:T(8,128)S(1)} async-done(((f32[8,22,256]{2,1,0:T(8,128)}), f32[8,22,256]{2,1,0:T(8,128)S(1)}, u32[]{:S(2)}, u32[]{:S(2)}) %all-to-all-start.1) | async-done | bytes 180256 | tf_op jit(solution)/shard_map/all_to_all | solution.py:76
  (51 shorter events, 5.4 us)
Async XLA Ops:
  7.2 18.5 %copy-start = (bf16[1,2,176,1024]{3,2,1,0:T(8,128)(2,1)S(1)}, bf16[1,2,176,1024]{3,2,1,0:T(8,128)(2,1)}, u32[]{:S(2)}) copy-start(bf16[1,2,176,1024]{3,2,1,0:T(8,128)(2,1)} %param.8) | copy-start | bytes 2162692
  7.2 78.0 %collective-permute-start.2 = (bf16[176,1024]{1,0:T(8,128)(2,1)}, bf16[176,1024]{1,0:T(8,128)(2,1)S(1)}, u32[]{:S(2)}, u32[]{:S(2)}) collective-permute-start(bf16[176,1024]{1,0:T(8,128)(2,1)} %bitcast.180), channel_id=1, source_target_pairs={{64,0},{128,64},{192,128},{256,192},{320,256},{384,320},{448,384},... | collective-permute-start | bytes 1081352 | tf_op jit(solution)/shard_map/ppermute | solution.py:13
  23.7 6.6 %collective-permute-start = (bf16[22,2048]{1,0:T(8,128)(2,1)S(1)}, bf16[22,2048]{1,0:T(8,128)(2,1)S(1)}, u32[]{:S(2)}, u32[]{:S(2)}) collective-permute-start(bf16[22,2048]{1,0:T(8,128)(2,1)S(1)} %reshape.163), channel_id=1, source_target_pairs={{448,0},{0,64},{64,128},{128,192},{192,256},{256,320},{320,384},{3... | collective-permute-start | bytes 270344 | tf_op jit(solution)/shard_map/ppermute | solution.py:13
  26.4 59.0 %collective-permute-start.1 = (bf16[176,1024]{1,0:T(8,128)(2,1)}, bf16[176,1024]{1,0:T(8,128)(2,1)S(1)}, u32[]{:S(2)}, u32[]{:S(2)}) collective-permute-start(bf16[176,1024]{1,0:T(8,128)(2,1)} %dynamic-slice_bitcast_fusion), channel_id=1, source_target_pairs={{448,0},{0,64},{64,128},{128,192},{192,256},{256,320},{320,384},{3... | collective-permute-start | bytes 1081352 | tf_op jit(solution)/shard_map/ppermute | solution.py:13
  31.0 12.3 %all-to-all-start = ((bf16[22,8,256]{2,0,1:T(8,128)(2,1)}), bf16[22,8,256]{2,0,1:T(8,128)(2,1)S(1)}, u32[]{:S(2)}, u32[]{:S(2)}) async-start(bf16[22,8,256]{2,0,1:T(8,128)(2,1)} %copy.96), calls=%async_computation | async-start | bytes 196608 | tf_op jit(solution)/shard_map/all_to_all | solution.py:41
  37.9 152.1 %reduce-scatter.4.cloned.1.call-start = ((), (), s32[]{:S(2)}) async-start(), calls=%async_computation.3 | async-start | bytes 1622016
  94.0 2.6 %copy-start.1 = (bf16[8,176,1408]{2,1,0:T(8,128)(2,1)}, bf16[8,176,1408]{2,1,0:T(8,128)(2,1)S(1)}, u32[]{:S(2)}) copy-start(bf16[8,176,1408]{2,1,0:T(8,128)(2,1)S(1)} %fusion.6) | copy-start | bytes 11894788
  193.0 13.5 %all-to-all-start.1 = ((f32[8,22,256]{2,1,0:T(8,128)}), f32[8,22,256]{2,1,0:T(8,128)S(1)}, u32[]{:S(2)}, u32[]{:S(2)}) async-start(f32[8,22,256]{2,1,0:T(8,128)} %copy.107), calls=%async_computation.1 | async-start | bytes 393216 | tf_op jit(solution)/shard_map/all_to_all | solution.py:76
Sparse Core Ops, SparseCore 0:
  98.4 91.6 reduce-scatter.3
